TPU v7x, 32 devices: a whole 2x2x4 slice. The times are simulated.
32 devices in a mesh: sub: 8 (over y, x, core), grp: 4 (over z).
Axes of the slice: x: 2, y: 2, z: 4, core: 2. Of those that a mesh axis runs over, the one named last changes fastest.
Arguments:
- gaps: float32 [4, 16, 96, 1024], P('grp', 'sub'), may hold values from -6 to 6
- dual_op: bfloat16 [4, 16, 1024, 1024], P('grp', 'sub'), may hold values from -1 to 2.5, as said below
- dirichlet: bfloat16 [4, 16, 1024, 1024], P('grp', 'sub'), may hold values from -1 to 2.5, as said below
- modes: float32 [4, 16, 6, 1024], P('grp', 'sub'), may hold values from -6 to 6
- coarse_op: float32 [4, 16, 6, 384], P('grp', 'sub'), may hold values from -0.0009765625 to 0.0009765625, as said below
- slot_map: int32 [4, 16, 1024], P('grp', 'sub'), may hold values from 0 to 1023, as said below
Outputs:
- multipliers: float32 [4, 16, 96, 1024], P('grp', 'sub')
- residual: float32 [4, 16, 96, 1024], P('grp', 'sub')
Inputs may be any that keep to these rules, and one draw needn't show every extreme that they name: `dual_op`: each subdomain's block is symmetric positive definite. `dirichlet`: each subdomain's block is symmetric positive definite. The 384 x 384 matrix whose row (16 y + x) * 6 + k is coarse_op[y, x, k] is symmetric. `slot_map`: for every subdomain and face f, the entries f * 256 to (f + 1) * 256 - 1 are a permutation of those same slot numbers.
All inputs are finite; a program needn't handle non-finite values.
Results may differ from a plain program's by a relative error of at most 0.012.
The roundings to bfloat16 on the way count: a program that leaves them out, or rounds other values in their place, can miss the bound.
Values sent between devices are 32-bit elements; how exact they have to be, the bound alone decides.
No kernel may reach another device: no remote copies, remote signals or barrier semaphores. Data moves between devices by JAX's collectives and lax.ppermute only.
A program may use at most 128 MiB of HBM per device.

v0:
```python
import jax
import jax.numpy as jnp
from jax import lax
from jax.sharding import PartitionSpec as P

MODES = 6
ITERS = 2
HIGHEST = lax.Precision.HIGHEST


def extended(block, sides, width):
    for axis, dim in sides:
        count = lax.axis_size(axis)
        forward = [(i, i + 1) for i in range(count - 1)]
        backward = [(target, source) for source, target in forward]
        low = lax.ppermute(
            lax.slice_in_dim(block, block.shape[dim] - width, None, axis=dim), axis, forward
        )
        high = lax.ppermute(lax.slice_in_dim(block, 0, width, axis=dim), axis, backward)
        block = jnp.concatenate([low, block, high], axis=dim)
    return block


def inverse_map(maps):
    width = maps.shape[-1]

    def invert(perm_row):
        return jnp.zeros_like(perm_row).at[perm_row].set(jnp.arange(width, dtype=jnp.int32))

    return jax.vmap(invert)(maps)


def reorder_block(matrix, order):
    rows_first = jnp.take(matrix, order, axis=0)
    swapped = jnp.swapaxes(rows_first, 0, 1)
    both = jnp.take(swapped, order, axis=0)
    return jnp.swapaxes(both, 0, 1)


def jump_local(values):
    subdomains, columns, width = values.shape
    faces = values.reshape(subdomains, columns, 4, width // 4)
    edges = jnp.stack([faces[0, :, 0], faces[-1, :, 1]])
    beside = extended(edges, (("sub", 0),), 1)
    rims = jnp.stack([faces[:, :, 2], faces[:, :, 3]])
    across = extended(rims, (("grp", 0),), 1)
    from_left = jnp.concatenate([beside[0][None], faces[:-1, :, 1]], axis=0)
    from_right = jnp.concatenate([faces[1:, :, 0], beside[3][None]], axis=0)
    partner = jnp.stack([from_left, from_right, across[0], across[3]], axis=2)
    return (faces - partner).reshape(subdomains, columns, width)


def apply_blocks(values, matrices):
    return jnp.einsum(
        "snm,smk->snk", values.astype(jnp.bfloat16), matrices, preferred_element_type=jnp.float32
    )


def shards(gaps, dual_op, dirichlet, modes, coarse_op, slot_map):
    maps = slot_map[0]
    back_map = inverse_map(maps)
    vectors = jnp.take_along_axis(gaps[0], maps[:, None, :], axis=2)
    subdomains, columns, width = vectors.shape
    quarter = width // 4
    sub_total = lax.axis_size("sub")
    grp_total = lax.axis_size("grp")
    x_position = lax.axis_index("sub") * subdomains + jnp.arange(subdomains, dtype=jnp.int32)
    grp_here = lax.axis_index("grp")
    filler = jnp.ones((subdomains,), jnp.float32)
    face_weight = jnp.stack(
        [
            jnp.where(x_position == 0, 1.0, 2.0) * filler,
            jnp.where(x_position == sub_total * subdomains - 1, 1.0, 2.0) * filler,
            jnp.where(grp_here == 0, 1.0, 2.0) * filler,
            jnp.where(grp_here == grp_total - 1, 1.0, 2.0) * filler,
        ],
        axis=1,
    )
    slot_weight = jnp.repeat(face_weight, quarter, axis=1)
    ordered_modes = jnp.take_along_axis(modes[0], maps[:, None, :], axis=2)
    weighted_modes = ordered_modes * slot_weight[:, None, :]
    stiffness = jax.vmap(reorder_block)(dual_op[0], maps)
    schur_blocks = jax.vmap(reorder_block)(dirichlet[0], maps)
    rows_here = coarse_op[0].reshape(subdomains * MODES, -1)
    rows_count = rows_here.shape[0]
    rows_sub_major = rows_here.reshape(rows_count, grp_total, sub_total, rows_count)
    rows_sub_major = rows_sub_major.transpose(0, 2, 1, 3).reshape(rows_count, -1)
    coarse_total = rows_here.shape[1]
    face_modes = ordered_modes.reshape(subdomains, MODES, 4, quarter).transpose(0, 2, 1, 3)
    own_rows = rows_here.reshape(subdomains, 1, MODES, coarse_total)
    packed = jnp.concatenate(
        [face_modes, jnp.broadcast_to(own_rows, (subdomains, 4, MODES, coarse_total))], axis=3
    )
    edge_pack = jnp.stack([packed[0, 0], packed[-1, 1]])
    beside_pack = extended(edge_pack, (("sub", 0),), 1)
    rim_pack = jnp.stack([packed[:, 2], packed[:, 3]])
    across_pack = extended(rim_pack, (("grp", 0),), 1)
    left_pack = jnp.concatenate([beside_pack[0][None], packed[:-1, 1]], axis=0)
    right_pack = jnp.concatenate([packed[1:, 0], beside_pack[3][None]], axis=0)
    partner_pack = jnp.stack([left_pack, right_pack, across_pack[0], across_pack[3]], axis=1)
    partner_modes = partner_pack[:, :, :, :quarter]
    partner_rows = partner_pack[:, :, :, quarter:]

    def coefficients(values):
        return jnp.einsum("skm,snm->skn", weighted_modes, values, precision=HIGHEST)

    def gathered(coeffs):
        grouped = lax.all_gather(coeffs[None], "grp", axis=0, tiled=True)
        everything = lax.all_gather(grouped, "sub", axis=1, tiled=True)
        return everything.reshape(-1, columns)

    def amounts_of(flat):
        return jnp.dot(rows_here, flat, precision=HIGHEST, preferred_element_type=jnp.float32)

    def lift(amounts, flat):
        shaped = amounts.reshape(subdomains, MODES, columns)
        own_face = jnp.einsum("sfkm,skn->snfm", face_modes, shaped, precision=HIGHEST)
        far_amounts = jnp.einsum("sfkc,cn->sfkn", partner_rows, flat, precision=HIGHEST)
        far_face = jnp.einsum("sfkm,sfkn->snfm", partner_modes, far_amounts, precision=HIGHEST)
        return (own_face - far_face).reshape(subdomains, columns, width)

    def project(values):
        flat = gathered(coefficients(values))
        return values - lift(amounts_of(flat), flat)

    dual = jump_local(vectors)
    multipliers = jnp.zeros_like(dual)
    residual = project(dual)
    direction = jnp.zeros_like(dual)
    rho_prev = jnp.ones((columns,), jnp.float32)
    for step_index in range(ITERS):
        projected = project(residual)
        precond = jump_local(apply_blocks(projected, schur_blocks))
        rho_now = lax.psum(jnp.sum(projected * precond, axis=(0, 2)), ("sub", "grp"))
        search = project(precond)
        if step_index > 0:
            search = search + (rho_now / rho_prev)[None, :, None] * direction
        direction = search
        image = jump_local(apply_blocks(direction, stiffness))
        partial_dot = jnp.sum(direction * image, axis=(0, 2))
        curvature = lax.psum(partial_dot, ("sub", "grp"))
        step_len = rho_now / curvature
        multipliers = multipliers + step_len[None, :, None] * direction
        residual = residual - step_len[None, :, None] * image
        rho_prev = rho_now
    multipliers = jnp.take_along_axis(multipliers, back_map[:, None, :], axis=2)
    residual = jnp.take_along_axis(residual, back_map[:, None, :], axis=2)
    return (multipliers[None], residual[None])


def solution(mesh):
    placed = (
        P("grp", "sub", None, None),
        P("grp", "sub", None, None),
        P("grp", "sub", None, None),
        P("grp", "sub", None, None),
        P("grp", "sub", None, None),
        P("grp", "sub", None),
    )
    return jax.shard_map(
        shards,
        mesh=mesh,
        in_specs=placed,
        out_specs=(P("grp", "sub", None, None), P("grp", "sub", None, None)),
        check_vma=False,
    )
```

profile of v0, /device:TPU:0, one launch (start us, length us, event | category | flops | bytes accessed | tf_op | source)
XLA Modules:
  0.0 632.0 jit_solution(5257530324860456469)
XLA Ops:
  2.6 13.0 %gather_fusion = f32[2048,6]{1,0:T(8,128)S(1)} fusion(f32[2,6,1024]{1,2,0:T(8,128)S(1)} %bitcast.393, s32[2048]{0:T(1024)S(1)} %get-tuple-element.61), kind=kCustom, calls=%fused_computation.7 | custom fusion | bytes 114688 | tf_op jit(solution)/shard_map/jit(take_along_axis)/gather | solution.py:80
  17.6 2.4 collective-permute-start.4
  19.9 1.3 collective-permute-start.5
  21.3 4.3 collective-permute-start.6
  25.6 1.3 collective-permute-start.7
  27.3 13.0 %gather_fusion.1 = f32[2048,96]{1,0:T(8,128)S(1)} fusion(f32[2,96,1024]{1,2,0:T(8,128)S(1)} %bitcast.378, s32[2048]{0:T(1024)S(1)} %bitcast.377), kind=kCustom, calls=%fused_computation.clone | custom fusion | bytes 1589248 | tf_op jit(solution)/shard_map/jit(take_along_axis)/gather | solution.py:62
  41.5 4.0 collective-permute-start
  46.2 42.2 %gather_fusion.2 = bf16[2048,1024]{1,0:T(8,128)(2,1)} fusion(bf16[2,1024,1024]{2,1,0:T(8,128)(2,1)} %bitcast.375, s32[2048]{0:T(1024)S(1)} %get-tuple-element.60), kind=kCustom, calls=%fused_computation.1.clone | custom fusion | bytes 8404992 | tf_op jit(solution)/shard_map/vmap(jit(_take))/gather | solution.py:34
  88.4 6.2 copy.139
  94.6 42.0 %gather_fusion.4 = bf16[2048,1024]{1,0:T(8,128)(2,1)} fusion(bf16[2,1024,1024]{2,1,0:T(8,128)(2,1)} %bitcast.376, s32[2048]{0:T(1024)S(1)} %get-tuple-element.60), kind=kCustom, calls=%fused_computation.5.clone | custom fusion | bytes 8404992 | tf_op jit(solution)/shard_map/vmap(jit(_take))/gather | solution.py:34
  136.6 6.3 copy.148
  143.1 8.0 %scatter_custom_fusion = s32[2048]{0:T(1024)S(1)} fusion(s32[2048]{0:T(1024)S(1)} %get-tuple-element.65, s32[2048]{0:T(1024)S(1)} %get-tuple-element.64, s32[]{:T(128)} %constant.29.clone.1), kind=kCustom, calls=%fused_computation.184 | custom fusion | bytes 8196
  151.3 7.5 %select_bitcast_fusion = (bf16[2,1024,1024]{2,1,0:T(8,128)(2,1)}, bf16[2,1024,1024]{2,1,0:T(8,128)(2,1)}) fusion(bf16[2,1024,1024]{1,2,0:T(8,128)(2,1)} %copy.148, pred[2,1024]{1,0:T(4,128)(4,1)S(1)} %compare_and_fusion.1, bf16[2,1024,1024]{1,2,0:T(8,128)(2,1)} %copy.139), kind=kLoop, calls=%fused_computation.9 | loop fusion | flops 4194304 | bytes 16779264 | tf_op jit(solution)/shard_map/vmap()/transpose | solution.py:35
  159.4 40.6 %gather_fusion.3 = bf16[2048,1024]{1,0:T(8,128)(2,1)} fusion(bf16[2,1024,1024]{2,1,0:T(8,128)(2,1)} %get-tuple-element.57, s32[2048]{0:T(1024)S(1)} %get-tuple-element.60), kind=kCustom, calls=%fused_computation.4.clone | custom fusion | bytes 8404992 | tf_op jit(solution)/shard_map/vmap(jit(_take))/gather | solution.py:36
  200.0 40.7 %gather_fusion.5 = bf16[2048,1024]{1,0:T(8,128)(2,1)} fusion(bf16[2,1024,1024]{2,1,0:T(8,128)(2,1)} %get-tuple-element.56, s32[2048]{0:T(1024)S(1)} %get-tuple-element.60), kind=kCustom, calls=%fused_computation.6.clone | custom fusion | bytes 8404992 | tf_op jit(solution)/shard_map/vmap(jit(_take))/gather | solution.py:36
  242.0 4.1 collective-permute-start.2
  246.2 1.5 collective-permute-start.3
  249.3 4.6 collective-permute-done.3
  255.9 13.5 %all-gather = f32[8,6,96]{2,1,0:T(8,128)S(1)} all-gather(f32[2,6,96]{2,1,0:T(8,128)S(1)} %fusion.40), channel_id=2, replica_groups=mesh['sub'=8,'grp'=4] {'grp'}, dimensions={0}, use_global_device_ids=true | all-gather | bytes 23040 | tf_op jit(solution)/shard_map/all_gather | solution.py:108
  269.5 13.7 %all_gather.31 = f32[4,16,6,96]{3,2,1,0:T(8,128)S(1)} all-gather(f32[4,2,6,96]{3,2,1,0:T(8,128)S(1)} %bitcast.410), channel_id=1, replica_groups=mesh['sub'=8,'grp'=4] {'sub'}, dimensions={1}, use_global_device_ids=true | all-gather | bytes 165888 | tf_op jit(solution)/shard_map/all_gather | solution.py:109
  286.4 13.1 %all-gather.1 = f32[8,6,96]{2,1,0:T(8,128)S(1)} all-gather(f32[2,6,96]{2,1,0:T(8,128)S(1)} %fusion.38), channel_id=3, replica_groups=mesh['sub'=8,'grp'=4] {'grp'}, dimensions={0}, use_global_device_ids=true | all-gather | bytes 23040 | tf_op jit(solution)/shard_map/all_gather | solution.py:108
  299.5 7.9 %all_gather.33 = f32[4,16,6,96]{3,2,1,0:T(8,128)S(1)} all-gather(f32[4,2,6,96]{3,2,1,0:T(8,128)S(1)} %bitcast.411), channel_id=1, replica_groups=mesh['sub'=8,'grp'=4] {'sub'}, dimensions={1}, use_global_device_ids=true | all-gather | bytes 165888 | tf_op jit(solution)/shard_map/all_gather | solution.py:109
  310.2 1.7 fusion.1
  312.6 2.3 collective-permute-start.8
  315.2 1.3 collective-permute-start.9
  316.5 1.5 collective-permute-start.10
  318.1 1.5 collective-permute-start.11
  320.4 1.4 collective-permute-done.10
  321.8 4.7 collective-permute-done.11
  327.7 1.4 multiply_reduce_fusion.3
  329.9 13.2 %all-gather.2 = f32[8,6,96]{2,1,0:T(8,128)S(1)} all-gather(f32[2,6,96]{2,1,0:T(8,128)S(1)} %fusion.36), channel_id=4, replica_groups=mesh['sub'=8,'grp'=4] {'grp'}, dimensions={0}, use_global_device_ids=true | all-gather | bytes 23040 | tf_op jit(solution)/shard_map/all_gather | solution.py:108
  343.0 11.7 %all_gather.35 = f32[4,16,6,96]{3,2,1,0:T(8,128)S(1)} all-gather(f32[4,2,6,96]{3,2,1,0:T(8,128)S(1)} %bitcast.412), channel_id=1, replica_groups=mesh['sub'=8,'grp'=4] {'sub'}, dimensions={1}, use_global_device_ids=true | all-gather | bytes 165888 | tf_op jit(solution)/shard_map/all_gather | solution.py:109
  357.5 1.8 fusion.3
  360.0 2.3 collective-permute-start.12
  362.6 1.3 collective-permute-start.13
  363.9 1.6 collective-permute-start.14
  367.6 3.0 collective-permute-done.14
  370.6 4.4 collective-permute-done.15
  377.1 1.7 multiply_reduce_fusion.2
  378.7 39.3 %all-reduce = (f32[96]{0:T(128)S(1)}, f32[96]{0:T(128)S(1)}) all-reduce(f32[96]{0:T(128)S(1)} %get-tuple-element.12, f32[96]{0:T(128)S(1)} %get-tuple-element.10), channel_id=1, replica_groups=mesh['sub'=8,'grp'=4] {'sub','grp'}, use_global_device_ids=true, to_apply=%region_1.4 | all-reduce | flops 192 | bytes 1536 | tf_op jit(solution)/shard_map/psum | solution.py:134
  419.0 13.1 %all-gather.3 = f32[8,6,96]{2,1,0:T(8,128)S(1)} all-gather(f32[2,6,96]{2,1,0:T(8,128)S(1)} %fusion.34), channel_id=5, replica_groups=mesh['sub'=8,'grp'=4] {'grp'}, dimensions={0}, use_global_device_ids=true | all-gather | bytes 23040 | tf_op jit(solution)/shard_map/all_gather | solution.py:108
  432.1 10.5 %all_gather.37 = f32[4,16,6,96]{3,2,1,0:T(8,128)S(1)} all-gather(f32[4,2,6,96]{3,2,1,0:T(8,128)S(1)} %bitcast.413), channel_id=1, replica_groups=mesh['sub'=8,'grp'=4] {'sub'}, dimensions={1}, use_global_device_ids=true | all-gather | bytes 165888 | tf_op jit(solution)/shard_map/all_gather | solution.py:109
  445.9 1.8 fusion
  448.4 2.3 collective-permute-start.16
  453.6 4.6 collective-permute-start.18
  459.0 2.3 collective-permute-done.19
  461.3 1.8 collective-permute-done.18
  463.8 1.3 stack.96
  465.1 1.9 multiply_reduce_fusion.1
  467.7 13.2 %all-gather.4 = f32[8,6,96]{2,1,0:T(8,128)S(1)} all-gather(f32[2,6,96]{2,1,0:T(8,128)S(1)} %fusion.32), channel_id=6, replica_groups=mesh['sub'=8,'grp'=4] {'grp'}, dimensions={0}, use_global_device_ids=true | all-gather | bytes 23040 | tf_op jit(solution)/shard_map/all_gather | solution.py:108
  480.9 10.2 %all_gather.39 = f32[4,16,6,96]{3,2,1,0:T(8,128)S(1)} all-gather(f32[4,2,6,96]{3,2,1,0:T(8,128)S(1)} %bitcast.414), channel_id=1, replica_groups=mesh['sub'=8,'grp'=4] {'sub'}, dimensions={1}, use_global_device_ids=true | all-gather | bytes 165888 | tf_op jit(solution)/shard_map/all_gather | solution.py:109
  491.7 38.7 %psum.30 = f32[96]{0:T(128)S(1)} all-reduce(f32[96]{0:T(128)S(1)} %get-tuple-element.8), channel_id=1, replica_groups=mesh['sub'=8,'grp'=4] {'sub','grp'}, use_global_device_ids=true, to_apply=%region_5.8 | all-reduce | flops 96 | bytes 768 | tf_op jit(solution)/shard_map/psum | solution.py:134
  532.6 2.5 fusion.2
  535.1 1.5 reshape.211
  536.9 1.3 collective-permute-start.20
  539.8 3.4 collective-permute-start.22
  546.4 4.4 collective-permute-done.23
  552.8 2.5 multiply_reduce_fusion
  555.4 43.3 %psum.31 = f32[96]{0:T(128)S(1)} all-reduce(f32[96]{0:T(128)S(1)} %get-tuple-element.6), channel_id=1, replica_groups=mesh['sub'=8,'grp'=4] {'sub','grp'}, use_global_device_ids=true, to_apply=%region_7.10 | all-reduce | flops 96 | bytes 768 | tf_op jit(solution)/shard_map/psum | solution.py:141
  598.7 2.3 multiply_subtract_fusion
  601.0 1.5 copy.169
  602.5 13.0 %gather_fusion.6 = f32[2048,96]{1,0:T(8,128)S(1)} fusion(f32[2,96,1024]{1,2,0:T(8,128)S(1)} %copy.169, s32[2048]{0:T(1024)S(1)} %bitcast.373), kind=kCustom, calls=%fused_computation.2.clone | custom fusion | bytes 1589248 | tf_op jit(solution)/shard_map/jit(take_along_axis)/gather | solution.py:146
  617.1 13.0 %gather_fusion.7 = f32[2048,96]{1,0:T(8,128)S(1)} fusion(f32[2,96,1024]{1,2,0:T(8,128)S(1)} %copy.171, s32[2048]{0:T(1024)S(1)} %bitcast.374), kind=kCustom, calls=%fused_computation.3.clone | custom fusion | bytes 1589248 | tf_op jit(solution)/shard_map/jit(take_along_axis)/gather | solution.py:147
  630.5 1.3 select_bitcast_fusion.2
  (192 shorter events, 50.8 us)
Async XLA Ops:
  0.6 26.3 %copy-start.10 = (s32[1,2,1024]{2,1,0:T(2,128)S(1)}, s32[1,2,1024]{2,1,0:T(2,128)}, u32[]{:S(2)}) copy-start(s32[1,2,1024]{2,1,0:T(2,128)} %param.15) | copy-start | bytes 24580
  0.6 26.3 %copy-start.9 = (f32[1,2,96,1024]{3,2,1,0:T(8,128)S(1)}, f32[1,2,96,1024]{3,2,1,0:T(8,128)}, u32[]{:S(2)}) copy-start(f32[1,2,96,1024]{3,2,1,0:T(8,128)} %param.10) | copy-start | bytes 2359300
  17.6 223.1 %collective-permute-start.4 = (f32[1,6,640]{2,1,0:T(8,128)S(1)}, f32[1,6,640]{2,1,0:T(8,128)S(1)}, u32[]{:S(2)}, u32[]{:S(2)}) collective-permute-start(f32[1,6,640]{2,1,0:T(8,128)S(1)} %get-tuple-element.44), channel_id=1, source_target_pairs={{0,4},{4,8},{8,12},{12,16},{16,20},{20,24},{24,28},{1,5},{5,9},{9,... | collective-permute-start | bytes 46088 | tf_op jit(solution)/shard_map/ppermute | solution.py:16
  19.9 222.1 %collective-permute-start.5 = (f32[1,6,640]{2,1,0:T(8,128)S(1)}, f32[1,6,640]{2,1,0:T(8,128)S(1)}, u32[]{:S(2)}, u32[]{:S(2)}) collective-permute-start(f32[1,6,640]{2,1,0:T(8,128)S(1)} %get-tuple-element.45), channel_id=1, source_target_pairs={{4,0},{8,4},{12,8},{16,12},{20,16},{24,20},{28,24},{5,1},{9,5},{13... | collective-permute-start | bytes 46088 | tf_op jit(solution)/shard_map/ppermute | solution.py:19
  21.3 224.9 %collective-permute-start.6 = (f32[1,2,6,640]{3,2,1,0:T(8,128)S(1)}, f32[1,2,6,640]{3,2,1,0:T(8,128)S(1)}, u32[]{:S(2)}, u32[]{:S(2)}) collective-permute-start(f32[1,2,6,640]{3,2,1,0:T(8,128)S(1)} %get-tuple-element.48), channel_id=1, source_target_pairs={{0,1},{1,2},{2,3},{4,5},{5,6},{6,7},{8,9},{9,10},{10,11},{12,13},{... | collective-permute-start | bytes 92168 | tf_op jit(solution)/shard_map/ppermute | solution.py:16
  25.6 222.0 %collective-permute-start.7 = (f32[1,2,6,640]{3,2,1,0:T(8,128)S(1)}, f32[1,2,6,640]{3,2,1,0:T(8,128)S(1)}, u32[]{:S(2)}, u32[]{:S(2)}) collective-permute-start(f32[1,2,6,640]{3,2,1,0:T(8,128)S(1)} %get-tuple-element.49), channel_id=1, source_target_pairs={{1,0},{2,1},{3,2},{5,4},{6,5},{7,6},{9,8},{10,9},{11,10},{13,12},{... | collective-permute-start | bytes 92168 | tf_op jit(solution)/shard_map/ppermute | solution.py:19
  41.5 206.2 %collective-permute-start = (f32[1,96,256]{2,0,1:T(1,128)S(1)}, f32[1,96,256]{2,0,1:T(1,128)S(1)}, u32[]{:S(2)}, u32[]{:S(2)}) collective-permute-start(f32[1,96,256]{2,0,1:T(1,128)S(1)} %get-tuple-element.38), channel_id=1, source_target_pairs={{0,4},{4,8},{8,12},{12,16},{16,20},{20,24},{24,28},{1,5},{5,9},{9,... | collective-permute-start | bytes 294920 | tf_op jit(solution)/shard_map/ppermute | solution.py:16
  45.9 105.4 %copy-start.12 = (pred[2,1024]{1,0:T(4,128)(4,1)}, pred[2,1024]{1,0:T(4,128)(4,1)S(1)}, u32[]{:S(2)}) copy-start(pred[2,1024]{1,0:T(4,128)(4,1)S(1)} %compare_and_fusion.1) | copy-start | bytes 6148
  136.6 6.3 copy-start.15
  136.6 6.4 %copy-start.16 = (s32[2]{0:T(128)S(1)}, s32[2]{0:T(128)}, u32[]{:S(2)}) copy-start(s32[2]{0:T(128)} %constant.70) | copy-start | bytes 28
  151.3 8.1 %copy-start.11 = (f32[1,2,6,384]{3,1,2,0:T(2,128)S(1)}, f32[1,2,6,384]{3,1,2,0:T(2,128)}, u32[]{:S(2)}) copy-start(f32[1,2,6,384]{3,1,2,0:T(2,128)} %param.14) | copy-start | bytes 55300
  240.7 7.4 %collective-permute-start.1 = (f32[1,96,256]{2,0,1:T(1,128)S(1)}, f32[1,96,256]{2,0,1:T(1,128)S(1)}, u32[]{:S(2)}, u32[]{:S(2)}) collective-permute-start(f32[1,96,256]{2,0,1:T(1,128)S(1)} %get-tuple-element.39), channel_id=1, source_target_pairs={{4,0},{8,4},{12,8},{16,12},{20,16},{24,20},{28,24},{5,1},{9,5},{13... | collective-permute-start | bytes 294920 | tf_op jit(solution)/shard_map/ppermute | solution.py:19
  242.0 7.3 %collective-permute-start.2 = (f32[1,2,96,256]{3,0,2,1:T(1,128)S(1)}, f32[1,2,96,256]{3,0,2,1:T(1,128)S(1)}, u32[]{:S(2)}, u32[]{:S(2)}) collective-permute-start(f32[1,2,96,256]{3,0,2,1:T(1,128)S(1)} %get-tuple-element.42), channel_id=1, source_target_pairs={{0,1},{1,2},{2,3},{4,5},{5,6},{6,7},{8,9},{9,10},{10,11},{12,13},{... | collective-permute-start | bytes 589832 | tf_op jit(solution)/shard_map/ppermute | solution.py:16
  246.2 7.7 %collective-permute-start.3 = (f32[1,2,96,256]{3,0,2,1:T(1,128)S(1)}, f32[1,2,96,256]{3,0,2,1:T(1,128)S(1)}, u32[]{:S(2)}, u32[]{:S(2)}) collective-permute-start(f32[1,2,96,256]{3,0,2,1:T(1,128)S(1)} %get-tuple-element.43), channel_id=1, source_target_pairs={{1,0},{2,1},{3,2},{5,4},{6,5},{7,6},{9,8},{10,9},{11,10},{13,12},{... | collective-permute-start | bytes 589832 | tf_op jit(solution)/shard_map/ppermute | solution.py:19
  285.6 24.2 %copy-start.13 = (pred[2,1024]{1,0:T(4,128)(4,1)S(1)}, pred[2,1024]{1,0:T(4,128)(4,1)}, u32[]{:S(2)}) copy-start(pred[2,1024]{1,0:T(4,128)(4,1)} %copy-done.12) | copy-start | bytes 6148
  308.0 2.2 copy-start.2
  309.9 2.4 copy-start.8
  312.6 7.0 %collective-permute-start.8 = (f32[1,96,256]{2,0,1:T(1,128)S(1)}, f32[1,96,256]{2,0,1:T(1,128)S(1)}, u32[]{:S(2)}, u32[]{:S(2)}) collective-permute-start(f32[1,96,256]{2,0,1:T(1,128)S(1)} %get-tuple-element.32), channel_id=1, source_target_pairs={{0,4},{4,8},{8,12},{12,16},{16,20},{20,24},{24,28},{1,5},{5,9},{9,... | collective-permute-start | bytes 294920 | tf_op jit(solution)/shard_map/ppermute | solution.py:16
  315.2 4.8 collective-permute-start.9
  316.5 5.3 collective-permute-start.10
  318.1 8.5 %collective-permute-start.11 = (f32[1,2,96,256]{3,0,2,1:T(1,128)S(1)}, f32[1,2,96,256]{3,0,2,1:T(1,128)S(1)}, u32[]{:S(2)}, u32[]{:S(2)}) collective-permute-start(f32[1,2,96,256]{3,0,2,1:T(1,128)S(1)} %get-tuple-element.37), channel_id=1, source_target_pairs={{1,0},{2,1},{3,2},{5,4},{6,5},{7,6},{9,8},{10,9},{11,10},{13,12},{... | collective-permute-start | bytes 589832 | tf_op jit(solution)/shard_map/ppermute | solution.py:19
  355.3 2.2 copy-start
  359.3 16.5 %copy-start.6 = (f32[2,96,1024]{2,1,0:T(8,128)}, f32[2,96,1024]{2,1,0:T(8,128)S(1)}, u32[]{:S(2)}) copy-start(f32[2,96,1024]{2,1,0:T(8,128)S(1)} %fusion.3) | copy-start | bytes 2359300
  360.0 6.9 %collective-permute-start.12 = (f32[1,96,256]{2,0,1:T(1,128)S(1)}, f32[1,96,256]{2,0,1:T(1,128)S(1)}, u32[]{:S(2)}, u32[]{:S(2)}) collective-permute-start(f32[1,96,256]{2,0,1:T(1,128)S(1)} %get-tuple-element.26), channel_id=1, source_target_pairs={{0,4},{4,8},{8,12},{12,16},{16,20},{20,24},{24,28},{1,5},{5,9},{9,... | collective-permute-start | bytes 294920 | tf_op jit(solution)/shard_map/ppermute | solution.py:16
  362.6 4.7 collective-permute-start.13
  363.9 6.7 %collective-permute-start.14 = (f32[1,2,96,256]{3,0,2,1:T(1,128)S(1)}, f32[1,2,96,256]{3,0,2,1:T(1,128)S(1)}, u32[]{:S(2)}, u32[]{:S(2)}) collective-permute-start(f32[1,2,96,256]{3,0,2,1:T(1,128)S(1)} %get-tuple-element.30), channel_id=1, source_target_pairs={{0,1},{1,2},{2,3},{4,5},{5,6},{6,7},{8,9},{9,10},{10,11},{12,13},{... | collective-permute-start | bytes 589832 | tf_op jit(solution)/shard_map/ppermute | solution.py:16
  365.5 9.5 %collective-permute-start.15 = (f32[1,2,96,256]{3,0,2,1:T(1,128)S(1)}, f32[1,2,96,256]{3,0,2,1:T(1,128)S(1)}, u32[]{:S(2)}, u32[]{:S(2)}) collective-permute-start(f32[1,2,96,256]{3,0,2,1:T(1,128)S(1)} %get-tuple-element.31), channel_id=1, source_target_pairs={{1,0},{2,1},{3,2},{5,4},{6,5},{7,6},{9,8},{10,9},{11,10},{13,12},{... | collective-permute-start | bytes 589832 | tf_op jit(solution)/shard_map/ppermute | solution.py:19
  443.1 2.8 copy-start.3
  445.0 0.9 copy-start.7
  447.7 16.1 %copy-start.5 = (f32[2,96,1024]{2,1,0:T(8,128)}, f32[2,96,1024]{2,1,0:T(8,128)S(1)}, u32[]{:S(2)}) copy-start(f32[2,96,1024]{2,1,0:T(8,128)S(1)} %fusion) | copy-start | bytes 2359300
  448.4 9.8 %collective-permute-start.16 = (f32[1,96,256]{2,0,1:T(1,128)S(1)}, f32[1,96,256]{2,0,1:T(1,128)S(1)}, u32[]{:S(2)}, u32[]{:S(2)}) collective-permute-start(f32[1,96,256]{2,0,1:T(1,128)S(1)} %get-tuple-element.20), channel_id=1, source_target_pairs={{0,4},{4,8},{8,12},{12,16},{16,20},{20,24},{24,28},{1,5},{5,9},{9,... | collective-permute-start | bytes 294920 | tf_op jit(solution)/shard_map/ppermute | solution.py:16
  451.0 7.6 %collective-permute-start.17 = (f32[1,96,256]{2,0,1:T(1,128)S(1)}, f32[1,96,256]{2,0,1:T(1,128)S(1)}, u32[]{:S(2)}, u32[]{:S(2)}) collective-permute-start(f32[1,96,256]{2,0,1:T(1,128)S(1)} %get-tuple-element.21), channel_id=1, source_target_pairs={{4,0},{8,4},{12,8},{16,12},{20,16},{24,20},{28,24},{5,1},{9,5},{13... | collective-permute-start | bytes 294920 | tf_op jit(solution)/shard_map/ppermute | solution.py:19
  452.3 9.0 %collective-permute-start.19 = (f32[1,2,96,256]{3,0,2,1:T(1,128)S(1)}, f32[1,2,96,256]{3,0,2,1:T(1,128)S(1)}, u32[]{:S(2)}, u32[]{:S(2)}) collective-permute-start(f32[1,2,96,256]{3,0,2,1:T(1,128)S(1)} %get-tuple-element.25), channel_id=1, source_target_pairs={{1,0},{2,1},{3,2},{5,4},{6,5},{7,6},{9,8},{10,9},{11,10},{13,12},{... | collective-permute-start | bytes 589832 | tf_op jit(solution)/shard_map/ppermute | solution.py:19
  453.6 9.5 %collective-permute-start.18 = (f32[1,2,96,256]{3,0,2,1:T(1,128)S(1)}, f32[1,2,96,256]{3,0,2,1:T(1,128)S(1)}, u32[]{:S(2)}, u32[]{:S(2)}) collective-permute-start(f32[1,2,96,256]{3,0,2,1:T(1,128)S(1)} %get-tuple-element.24), channel_id=1, source_target_pairs={{0,1},{1,2},{2,3},{4,5},{5,6},{6,7},{8,9},{9,10},{10,11},{12,13},{... | collective-permute-start | bytes 589832 | tf_op jit(solution)/shard_map/ppermute | solution.py:16
  530.4 2.2 copy-start.1
  536.9 7.7 %collective-permute-start.20 = (f32[1,96,256]{2,0,1:T(1,128)S(1)}, f32[1,96,256]{2,0,1:T(1,128)S(1)}, u32[]{:S(2)}, u32[]{:S(2)}) collective-permute-start(f32[1,96,256]{2,0,1:T(1,128)S(1)} %get-tuple-element.14), channel_id=1, source_target_pairs={{0,4},{4,8},{8,12},{12,16},{16,20},{20,24},{24,28},{1,5},{5,9},{9,... | collective-permute-start | bytes 294920 | tf_op jit(solution)/shard_map/ppermute | solution.py:16
  538.5 6.5 %collective-permute-start.21 = (f32[1,96,256]{2,0,1:T(1,128)S(1)}, f32[1,96,256]{2,0,1:T(1,128)S(1)}, u32[]{:S(2)}, u32[]{:S(2)}) collective-permute-start(f32[1,96,256]{2,0,1:T(1,128)S(1)} %get-tuple-element.15), channel_id=1, source_target_pairs={{4,0},{8,4},{12,8},{16,12},{20,16},{24,20},{28,24},{5,1},{9,5},{13... | collective-permute-start | bytes 294920 | tf_op jit(solution)/shard_map/ppermute | solution.py:19
  539.8 6.6 %collective-permute-start.22 = (f32[1,2,96,256]{3,0,2,1:T(1,128)S(1)}, f32[1,2,96,256]{3,0,2,1:T(1,128)S(1)}, u32[]{:S(2)}, u32[]{:S(2)}) collective-permute-start(f32[1,2,96,256]{3,0,2,1:T(1,128)S(1)} %get-tuple-element.18), channel_id=1, source_target_pairs={{0,1},{1,2},{2,3},{4,5},{5,6},{6,7},{8,9},{9,10},{10,11},{12,13},{... | collective-permute-start | bytes 589832 | tf_op jit(solution)/shard_map/ppermute | solution.py:16
  543.3 7.6 %collective-permute-start.23 = (f32[1,2,96,256]{3,0,2,1:T(1,128)S(1)}, f32[1,2,96,256]{3,0,2,1:T(1,128)S(1)}, u32[]{:S(2)}, u32[]{:S(2)}) collective-permute-start(f32[1,2,96,256]{3,0,2,1:T(1,128)S(1)} %get-tuple-element.19), channel_id=1, source_target_pairs={{1,0},{2,1},{3,2},{5,4},{6,5},{7,6},{9,8},{10,9},{11,10},{13,12},{... | collective-permute-start | bytes 589832 | tf_op jit(solution)/shard_map/ppermute | solution.py:19
  617.1 13.4 %copy-start.4 = (f32[2,1024,96]{1,2,0:T(8,128)S(1)}, f32[2,1024,96]{1,2,0:T(8,128)}, u32[]{:S(2)}) copy-start(f32[2,1024,96]{1,2,0:T(8,128)} %copy.170) | copy-start | bytes 2359300
  617.1 13.4 %copy-start.14 = (pred[2,1024]{1,0:T(4,128)(4,1)S(1)}, pred[2,1024]{1,0:T(4,128)(4,1)}, u32[]{:S(2)}) copy-start(pred[2,1024]{1,0:T(4,128)(4,1)} %and_bitcast_fusion) | copy-start | bytes 6148
where the time goes:
time: 644 us; the launch traced here: 632 us
  local copies, waits for them, and re-layouts  260 us (40%)
  blocking collectives  241 us (37%)
  starting transfers between devices  49.9 us (8%)
  waiting for transfers between devices  28.5 us (4%)
  other arithmetic  27.6 us (4%)
  matrix products  22.5 us (3%)
    gather x5, local copies, waits for them, and re-layouts, reorder_block(): rows_first = jnp.take(matrix, order, axis=0)  96.7 us
    gather x2, local copies, waits for them, and re-layouts, reorder_block(): both = jnp.take(swapped, order, axis=0)  81.3 us
    psum x2, blocking collectives, shards(): lax.psum(jnp.sum(projected * precond, axis=(0, 2)), ('sub', 'grp'))  78 us
    all_gather x5, blocking collectives, gathered(): grouped = lax.all_gather(coeffs[None], 'grp', axis=0, tiled=True)  66.2 us
    all_gather x5, blocking collectives, gathered(): everything = lax.all_gather(grouped, 'sub', axis=1, tiled=True)  53.9 us
    psum x1, blocking collectives, shards(): curvature = lax.psum(partial_dot, ('sub', 'grp'))  43.3 us
    ppermute x12, starting transfers between devices, extended(): lax.ppermute(lax.slice_in_dim(block, block.shape[dim] - width, None, axis...  34 us
    ppermute x12, waiting for transfers between devices, extended(): lax.ppermute(lax.slice_in_dim(block, 0, width, axis=dim), axis, backward)  20.5 us
  transfers between devices with their start and end apart: 24, of which 10 were waited for; matrix products, arithmetic and copies ran while one was open for 34% of the time, Pallas kernels for 0%

commit v1 on v0

--- a/solution.py
+++ b/solution.py
@@ -6,6 +6,28 @@
 MODES = 6
 ITERS = 2
 HIGHEST = lax.Precision.HIGHEST
+
+
+def joined_along(blocks, dim):
+    blocks = jnp.moveaxis(blocks, 0, dim)
+    shape = blocks.shape
+    return blocks.reshape(*shape[:dim], shape[dim] * shape[dim + 1], *shape[dim + 2 :])
+
+
+def ring_gather(shard, axis, dim):
+    count = lax.axis_size(axis)
+    pairs = [(i, (i + 1) % count) for i in range(count)]
+    back = [(b, a) for a, b in pairs]
+    lower, upper = ([], [])
+    for step in range(count - 1):
+        if step % 2 == 0:
+            lower.append(lax.ppermute(lower[-1] if lower else shard, axis, pairs))
+        else:
+            upper.append(lax.ppermute(upper[-1] if upper else shard, axis, back))
+    blocks = jnp.stack([*lower[::-1], shard, *upper])
+    shift = lax.axis_index(axis) - len(lower)
+    blocks = blocks[(jnp.arange(count) - shift) % count]
+    return joined_along(blocks, dim)
 
 
 def extended(block, sides, width):
@@ -105,7 +127,7 @@
         return jnp.einsum("skm,snm->skn", weighted_modes, values, precision=HIGHEST)
 
     def gathered(coeffs):
-        grouped = lax.all_gather(coeffs[None], "grp", axis=0, tiled=True)
+        grouped = ring_gather(coeffs[None], "grp", 0)
         everything = lax.all_gather(grouped, "sub", axis=1, tiled=True)
         return everything.reshape(-1, columns)
 

time: 644 us -> 622 us (0.966)
  blocking collectives: 241 us -> 172 us
  starting transfers between devices: 49.9 us -> 74.5 us
  waiting for transfers between devices: 28.5 us -> 40.4 us
    all_gather x5 -> x0, blocking collectives: 66.2 us -> none  [gathered(): grouped = lax.all_gather(coeffs[None], 'grp', axis=0, tiled=True)]
    ppermute x0 -> x15, starting transfers between devices: none -> 22.7 us  [the longest x10 12.2 us: ring_gather(): lower.append(lax.ppermute(lower[-1] if lower else shard, axis, pairs))]
    ppermute x0 -> x15, waiting for transfers between devices: none -> 10.1 us  [the longest x10 10 us: ring_gather(): lower.append(lax.ppermute(lower[-1] if lower else shard, axis, pairs))]
  transfers between devices with their start and end apart: 24 -> 39, of which waited for: 10 -> 15; matrix products, arithmetic and copies ran while one was open for 34% -> 36% of each run, Pallas kernels for 0% -> 0%
where the time goes in v1:
time: 622 us; the launch traced here: 610 us
  local copies, waits for them, and re-layouts  265 us (43%)
  blocking collectives  172 us (28%)
  starting transfers between devices  74.5 us (12%)
  waiting for transfers between devices  40.4 us (6%)
  other arithmetic  32.5 us (5%)
  matrix products  22.4 us (4%)
    gather x5, local copies, waits for them, and re-layouts, reorder_block(): rows_first = jnp.take(matrix, order, axis=0)  96.6 us
    gather x2, local copies, waits for them, and re-layouts, reorder_block(): both = jnp.take(swapped, order, axis=0)  81.4 us
    psum x2, blocking collectives, shards(): lax.psum(jnp.sum(projected * precond, axis=(0, 2)), ('sub', 'grp'))  78.9 us
    all_gather x5, blocking collectives, gathered(): everything = lax.all_gather(grouped, 'sub', axis=1, tiled=True)  52.1 us
    psum x1, blocking collectives, shards(): curvature = lax.psum(partial_dot, ('sub', 'grp'))  41 us
    ppermute x12, starting transfers between devices, extended(): lax.ppermute(lax.slice_in_dim(block, block.shape[dim] - width, None, axis...  36.1 us
    ppermute x12, waiting for transfers between devices, extended(): lax.ppermute(lax.slice_in_dim(block, 0, width, axis=dim), axis, backward)  21.9 us
    ppermute x12, starting transfers between devices, extended(): lax.ppermute(lax.slice_in_dim(block, 0, width, axis=dim), axis, backward)  15.7 us
  transfers between devices with their start and end apart: 39, of which 15 were waited for; matrix products, arithmetic and copies ran while one was open for 36% of the time, Pallas kernels for 0%

profile of v1, /device:TPU:0, one launch (start us, length us, event | category | flops | bytes accessed | tf_op | source)
XLA Modules:
  0.0 609.5 jit_solution(8832483640341701977)
XLA Ops:
  2.7 1.5 copy.54
  4.1 13.0 %gather_fusion.6 = f32[2048,96]{1,0:T(8,128)S(1)} fusion(f32[2,96,1024]{1,2,0:T(8,128)S(1)} %bitcast.410, s32[2048]{0:T(1024)S(1)} %bitcast.409), kind=kCustom, calls=%fused_computation.clone | custom fusion | bytes 1589248 | tf_op jit(solution)/shard_map/jit(take_along_axis)/gather | solution.py:84
  19.0 2.4 collective-permute-start
  23.7 5.0 collective-permute-start.2
  30.4 13.0 %gather_fusion.5 = f32[2048,6]{1,0:T(8,128)S(1)} fusion(f32[2,6,1024]{1,2,0:T(8,128)S(1)} %bitcast.425, s32[2048]{0:T(1024)S(1)} %get-tuple-element.61), kind=kCustom, calls=%fused_computation.12 | custom fusion | bytes 114688 | tf_op jit(solution)/shard_map/jit(take_along_axis)/gather | solution.py:102
  44.0 4.0 collective-permute-start.7
  49.1 42.1 %gather_fusion.7 = bf16[2048,1024]{1,0:T(8,128)(2,1)} fusion(bf16[2,1024,1024]{2,1,0:T(8,128)(2,1)} %bitcast.407, s32[2048]{0:T(1024)S(1)} %get-tuple-element.60), kind=kCustom, calls=%fused_computation.1.clone | custom fusion | bytes 8404992 | tf_op jit(solution)/shard_map/vmap(jit(_take))/gather | solution.py:56
  91.2 6.2 %copy.80 = bf16[2,1024,1024]{1,2,0:T(8,128)(2,1)} copy(bf16[2,1024,1024]{2,1,0:T(8,128)(2,1)} %bitcast.411) | data formatting | bytes 8388608 | tf_op jit(solution)/shard_map/vmap(jit(_take))/gather | solution.py:56
  97.4 42.1 %gather_fusion.9 = bf16[2048,1024]{1,0:T(8,128)(2,1)} fusion(bf16[2,1024,1024]{2,1,0:T(8,128)(2,1)} %bitcast.408, s32[2048]{0:T(1024)S(1)} %get-tuple-element.60), kind=kCustom, calls=%fused_computation.5.clone | custom fusion | bytes 8404992 | tf_op jit(solution)/shard_map/vmap(jit(_take))/gather | solution.py:56
  139.4 6.2 %copy.88 = bf16[2,1024,1024]{1,2,0:T(8,128)(2,1)} copy(bf16[2,1024,1024]{2,1,0:T(8,128)(2,1)} %bitcast.412) | data formatting | bytes 8388608 | tf_op jit(solution)/shard_map/vmap(jit(_take))/gather | solution.py:56
  147.0 3.3 collective-permute-done.8
  150.3 5.2 collective-permute-start.9
  159.1 1.7 pad_maximum_fusion
  162.1 2.7 collective-permute-start.4
  165.6 2.1 collective-permute-start.6
  169.3 4.5 collective-permute-done.5
  174.4 12.2 %all-gather = f32[4,16,6,96]{3,2,1,0:T(8,128)S(1)} all-gather(f32[4,2,6,96]{3,2,1,0:T(8,128)S(1)} %gather_fusion), channel_id=2, replica_groups=mesh['sub'=8,'grp'=4] {'sub'}, dimensions={1}, use_global_device_ids=true | all-gather | bytes 165888 | tf_op jit(solution)/shard_map/all_gather | solution.py:131
  190.0 6.1 %select_bitcast_fusion = (bf16[2,1024,1024]{2,1,0:T(8,128)(2,1)}, bf16[2,1024,1024]{2,1,0:T(8,128)(2,1)}) fusion(bf16[2,1024,1024]{1,2,0:T(8,128)(2,1)} %copy.88, pred[2,1024]{1,0:T(4,128)(4,1)S(1)} %copy-done.17, bf16[2,1024,1024]{1,2,0:T(8,128)(2,1)S(1)} %copy-done), kind=kLoop, calls=%fused_computation.14 | loop fusion | flops 4194304 | bytes 16779264 | tf_op jit(solution)/shard_map/vmap()/transpose | solution.py:57
  196.1 3.8 collective-permute-start.13
  200.6 40.8 %gather_fusion.8 = bf16[2048,1024]{1,0:T(8,128)(2,1)} fusion(bf16[2,1024,1024]{2,1,0:T(8,128)(2,1)} %get-tuple-element.57, s32[2048]{0:T(1024)S(1)} %get-tuple-element.60), kind=kCustom, calls=%fused_computation.4.clone | custom fusion | bytes 8404992 | tf_op jit(solution)/shard_map/vmap(jit(_take))/gather | solution.py:58
  242.1 7.9 %all-gather.1 = f32[4,16,6,96]{3,2,1,0:T(8,128)S(1)} all-gather(f32[4,2,6,96]{3,2,1,0:T(8,128)S(1)} %gather_fusion.1), channel_id=3, replica_groups=mesh['sub'=8,'grp'=4] {'sub'}, dimensions={1}, use_global_device_ids=true | all-gather | bytes 165888 | tf_op jit(solution)/shard_map/all_gather | solution.py:131
  252.8 1.7 fusion.1
  255.2 2.3 collective-permute-start.14
  260.4 1.5 collective-permute-start.17
  264.0 4.7 collective-permute-done.17
  269.8 2.0 multiply_reduce_fusion.3
  272.6 4.0 collective-permute-start.18
  277.5 1.5 collective-permute-done.18
  280.9 40.7 %gather_fusion.10 = bf16[2048,1024]{1,0:T(8,128)(2,1)} fusion(bf16[2,1024,1024]{2,1,0:T(8,128)(2,1)} %get-tuple-element.56, s32[2048]{0:T(1024)S(1)} %get-tuple-element.60), kind=kCustom, calls=%fused_computation.6.clone | custom fusion | bytes 8404992 | tf_op jit(solution)/shard_map/vmap(jit(_take))/gather | solution.py:58
  322.2 11.6 %all-gather.2 = f32[4,16,6,96]{3,2,1,0:T(8,128)S(1)} all-gather(f32[4,2,6,96]{3,2,1,0:T(8,128)S(1)} %gather_fusion.2), channel_id=4, replica_groups=mesh['sub'=8,'grp'=4] {'sub'}, dimensions={1}, use_global_device_ids=true | all-gather | bytes 165888 | tf_op jit(solution)/shard_map/all_gather | solution.py:131
  336.7 1.7 fusion.3
  339.1 2.3 collective-permute-start.21
  343.0 3.9 collective-permute-start.23
  349.0 3.0 collective-permute-done.23
  352.0 4.4 collective-permute-done.24
  359.9 38.4 %all-reduce = (f32[96]{0:T(128)S(1)}, f32[96]{0:T(128)S(1)}) all-reduce(f32[96]{0:T(128)S(1)} %copy-done.25, f32[96]{0:T(128)S(1)} %get-tuple-element.10), channel_id=1, replica_groups=mesh['sub'=8,'grp'=4] {'sub','grp'}, use_global_device_ids=true, to_apply=%region_1.4 | all-reduce | flops 192 | bytes 1536 | tf_op jit(solution)/shard_map/psum | solution.py:156
  399.8 1.8 collective-permute-start.25
  401.6 2.1 collective-permute-start.27
  403.6 1.7 collective-permute-done.25
  405.3 8.0 %scatter_custom_fusion = s32[2048]{0:T(1024)S(1)} fusion(s32[2048]{0:T(1024)S(1)} %get-tuple-element.65, s32[2048]{0:T(1024)S(1)} %get-tuple-element.64, s32[]{:T(128)} %constant.75.clone.1), kind=kCustom, calls=%fused_computation.195 | custom fusion | bytes 8196
  414.1 10.1 %all-gather.3 = f32[4,16,6,96]{3,2,1,0:T(8,128)S(1)} all-gather(f32[4,2,6,96]{3,2,1,0:T(8,128)S(1)} %gather_fusion.3), channel_id=5, replica_groups=mesh['sub'=8,'grp'=4] {'sub'}, dimensions={1}, use_global_device_ids=true | all-gather | bytes 165888 | tf_op jit(solution)/shard_map/all_gather | solution.py:131
  427.6 1.7 fusion
  430.0 2.2 collective-permute-start.28
  433.9 2.5 collective-permute-start.30
  438.5 2.4 collective-permute-done.30
  441.0 4.7 collective-permute-done.31
  447.8 1.9 multiply_reduce_fusion.1
  450.4 2.1 collective-permute-start.32
  452.5 1.8 collective-permute-start.34
  454.3 1.6 collective-permute-done.32
  456.3 40.5 %psum.30 = f32[96]{0:T(128)S(1)} all-reduce(f32[96]{0:T(128)S(1)} %get-tuple-element.8), channel_id=1, replica_groups=mesh['sub'=8,'grp'=4] {'sub','grp'}, use_global_device_ids=true, to_apply=%region_5.8 | all-reduce | flops 96 | bytes 768 | tf_op jit(solution)/shard_map/psum | solution.py:156
  497.9 10.3 %all-gather.4 = f32[4,16,6,96]{3,2,1,0:T(8,128)S(1)} all-gather(f32[4,2,6,96]{3,2,1,0:T(8,128)S(1)} %gather_fusion.4), channel_id=6, replica_groups=mesh['sub'=8,'grp'=4] {'sub'}, dimensions={1}, use_global_device_ids=true | all-gather | bytes 165888 | tf_op jit(solution)/shard_map/all_gather | solution.py:131
  511.0 2.5 fusion.2
  513.4 1.5 reshape.280
  515.3 2.3 collective-permute-start.35
  519.2 2.9 collective-permute-start.37
  524.3 1.7 collective-permute-done.37
  526.0 4.7 collective-permute-done.38
  532.7 2.5 multiply_reduce_fusion
  535.2 41.0 %psum.31 = f32[96]{0:T(128)S(1)} all-reduce(f32[96]{0:T(128)S(1)} %get-tuple-element.6), channel_id=1, replica_groups=mesh['sub'=8,'grp'=4] {'sub','grp'}, use_global_device_ids=true, to_apply=%region_7.10 | all-reduce | flops 96 | bytes 768 | tf_op jit(solution)/shard_map/psum | solution.py:163
  576.3 2.3 multiply_subtract_fusion
  578.6 1.5 copy.107
  580.0 13.0 %gather_fusion.11 = f32[2048,96]{1,0:T(8,128)S(1)} fusion(f32[2,96,1024]{1,2,0:T(8,128)S(1)} %copy.107, s32[2048]{0:T(1024)S(1)} %bitcast.405), kind=kCustom, calls=%fused_computation.2.clone | custom fusion | bytes 1589248 | tf_op jit(solution)/shard_map/jit(take_along_axis)/gather | solution.py:168
  594.7 13.0 %gather_fusion.12 = f32[2048,96]{1,0:T(8,128)S(1)} fusion(f32[2,96,1024]{1,2,0:T(8,128)S(1)} %copy.109, s32[2048]{0:T(1024)S(1)} %bitcast.406), kind=kCustom, calls=%fused_computation.3.clone | custom fusion | bytes 1589248 | tf_op jit(solution)/shard_map/jit(take_along_axis)/gather | solution.py:169
  (260 shorter events, 73.4 us)
Async XLA Ops:
  17.2 12.8 %copy-start.15 = (f32[1,2,6,1024]{3,1,2,0:T(2,128)S(1)}, f32[1,2,6,1024]{3,1,2,0:T(2,128)}, u32[]{:S(2)}) copy-start(f32[1,2,6,1024]{3,1,2,0:T(2,128)} %param.13) | copy-start | bytes 147460
  17.5 26.3 %copy-start.10 = (s32[1,2,1024]{2,1,0:T(2,128)S(1)}, s32[1,2,1024]{2,1,0:T(2,128)}, u32[]{:S(2)}) copy-start(s32[1,2,1024]{2,1,0:T(2,128)} %param.15) | copy-start | bytes 24580
  17.5 26.3 %copy-start.14 = (f32[1,2,6,384]{3,1,2,0:T(2,128)S(1)}, f32[1,2,6,384]{3,1,2,0:T(2,128)}, u32[]{:S(2)}) copy-start(f32[1,2,6,384]{3,1,2,0:T(2,128)} %param.14) | copy-start | bytes 55300
  19.0 137.1 %collective-permute-start = (f32[1,96,256]{2,0,1:T(1,128)S(1)}, f32[1,96,256]{2,0,1:T(1,128)S(1)}, u32[]{:S(2)}, u32[]{:S(2)}) collective-permute-start(f32[1,96,256]{2,0,1:T(1,128)S(1)} %get-tuple-element.38), channel_id=1, source_target_pairs={{0,4},{4,8},{8,12},{12,16},{16,20},{20,24},{24,28},{1,5},{5,9},{9,... | collective-permute-start | bytes 294920 | tf_op jit(solution)/shard_map/ppermute | solution.py:38
  21.3 136.4 %collective-permute-start.1 = (f32[1,96,256]{2,0,1:T(1,128)}, f32[1,96,256]{2,0,1:T(1,128)}, u32[]{:S(2)}, u32[]{:S(2)}) collective-permute-start(f32[1,96,256]{2,0,1:T(1,128)} %get-tuple-element.39), channel_id=1, source_target_pairs={{4,0},{8,4},{12,8},{16,12},{20,16},{24,20},{28,24},{5,1},{9,5},{13... | collective-permute-start | bytes 294920 | tf_op jit(solution)/shard_map/ppermute | solution.py:41
  23.7 135.3 %collective-permute-start.2 = (f32[1,2,96,256]{3,0,2,1:T(1,128)}, f32[1,2,96,256]{3,0,2,1:T(1,128)}, u32[]{:S(2)}, u32[]{:S(2)}) collective-permute-start(f32[1,2,96,256]{3,0,2,1:T(1,128)} %get-tuple-element.42), channel_id=1, source_target_pairs={{0,1},{1,2},{2,3},{4,5},{5,6},{6,7},{8,9},{9,10},{10,11},{12,13},{... | collective-permute-start | bytes 589832 | tf_op jit(solution)/shard_map/ppermute | solution.py:38
  28.7 130.4 %collective-permute-start.3 = (f32[1,2,96,256]{3,0,2,1:T(1,128)}, f32[1,2,96,256]{3,0,2,1:T(1,128)}, u32[]{:S(2)}, u32[]{:S(2)}) collective-permute-start(f32[1,2,96,256]{3,0,2,1:T(1,128)} %get-tuple-element.43), channel_id=1, source_target_pairs={{1,0},{2,1},{3,2},{5,4},{6,5},{7,6},{9,8},{10,9},{11,10},{13,12},{... | collective-permute-start | bytes 589832 | tf_op jit(solution)/shard_map/ppermute | solution.py:41
  44.0 101.7 %collective-permute-start.7 = (f32[1,6,640]{2,1,0:T(8,128)S(1)}, f32[1,6,640]{2,1,0:T(8,128)S(1)}, u32[]{:S(2)}, u32[]{:S(2)}) collective-permute-start(f32[1,6,640]{2,1,0:T(8,128)S(1)} %get-tuple-element.44), channel_id=1, source_target_pairs={{0,4},{4,8},{8,12},{12,16},{16,20},{20,24},{24,28},{1,5},{5,9},{9,... | collective-permute-start | bytes 46088 | tf_op jit(solution)/shard_map/ppermute | solution.py:38
  48.0 43.1 %copy-start.16 = (pred[2,1024]{1,0:T(4,128)(4,1)}, pred[2,1024]{1,0:T(4,128)(4,1)S(1)}, u32[]{:S(2)}) copy-start(pred[2,1024]{1,0:T(4,128)(4,1)S(1)} %compare_and_fusion.1) | copy-start | bytes 6148
  49.0 124.8 %copy-start.20 = (s32[1024]{0:T(1024)}, s32[1024]{0:T(1024)S(1)}, u32[]{:S(2)}) copy-start(s32[1024]{0:T(1024)S(1)} %pad_clamp_fusion) | copy-start | bytes 12292
  145.7 4.6 collective-permute-start.8
  150.3 14.5 %collective-permute-start.9 = (f32[1,2,6,640]{3,2,1,0:T(8,128)}, f32[1,2,6,640]{3,2,1,0:T(8,128)}, u32[]{:S(2)}, u32[]{:S(2)}) collective-permute-start(f32[1,2,6,640]{3,2,1,0:T(8,128)} %get-tuple-element.48), channel_id=1, source_target_pairs={{0,1},{1,2},{2,3},{4,5},{5,6},{6,7},{8,9},{9,10},{10,11},{12,13},{... | collective-permute-start | bytes 92168 | tf_op jit(solution)/shard_map/ppermute | solution.py:38
  156.1 8.7 %collective-permute-start.10 = (f32[1,2,6,640]{3,2,1,0:T(8,128)}, f32[1,2,6,640]{3,2,1,0:T(8,128)}, u32[]{:S(2)}, u32[]{:S(2)}) collective-permute-start(f32[1,2,6,640]{3,2,1,0:T(8,128)} %get-tuple-element.49), channel_id=1, source_target_pairs={{1,0},{2,1},{3,2},{5,4},{6,5},{7,6},{9,8},{10,9},{11,10},{13,12},{... | collective-permute-start | bytes 92168 | tf_op jit(solution)/shard_map/ppermute | solution.py:41
  160.8 4.0 copy-start.9
  162.1 6.3 %collective-permute-start.4 = (f32[1,2,6,96]{3,2,1,0:T(8,128)S(1)}, f32[1,2,6,96]{3,2,1,0:T(8,128)S(1)}, u32[]{:S(2)}, u32[]{:S(2)}) collective-permute-start(f32[1,2,6,96]{3,2,1,0:T(8,128)S(1)} %bitcast.438), channel_id=1, source_target_pairs={{0,1},{1,2},{2,3},{3,0},{4,5},{5,6},{6,7},{7,4},{8,9},{9,10},{10,1... | collective-permute-start | bytes 13832 | tf_op jit(solution)/shard_map/ppermute | solution.py:24
  165.6 3.7 collective-permute-start.6
  168.4 5.4 collective-permute-start.5
  186.7 3.3 copy-start.17
  187.0 3.0 copy-start
  189.9 10.0 %copy-start.11 = (s32[2,1024,1]{1,0,2:T(2,128)S(1)}, s32[2,1024,1]{1,0,2:T(2,128)}, u32[]{:S(2)}) copy-start(s32[2,1024,1]{1,0,2:T(2,128)} %get-tuple-element.50) | copy-start | bytes 24580
  189.9 10.0 %copy-start.24 = (s32[2]{0:T(128)S(1)}, s32[2]{0:T(128)}, u32[]{:S(2)}) copy-start(s32[2]{0:T(128)} %constant.99) | copy-start | bytes 28
  189.9 10.0 %collective-permute-start.11 = (f32[1,2,6,96]{3,2,1,0:T(8,128)S(1)}, f32[1,2,6,96]{3,2,1,0:T(8,128)S(1)}, u32[]{:S(2)}, u32[]{:S(2)}) collective-permute-start(f32[1,2,6,96]{3,2,1,0:T(8,128)S(1)} %bitcast.444), channel_id=1, source_target_pairs={{0,1},{1,2},{2,3},{3,0},{4,5},{5,6},{6,7},{7,4},{8,9},{9,10},{10,1... | collective-permute-start | bytes 13832 | tf_op jit(solution)/shard_map/ppermute | solution.py:24
  196.1 45.3 %collective-permute-start.13 = (f32[1,2,6,96]{3,2,1,0:T(8,128)S(1)}, f32[1,2,6,96]{3,2,1,0:T(8,128)S(1)}, u32[]{:S(2)}, u32[]{:S(2)}) collective-permute-start(f32[1,2,6,96]{3,2,1,0:T(8,128)S(1)} %bitcast.445), channel_id=1, source_target_pairs={{1,0},{2,1},{3,2},{0,3},{5,4},{6,5},{7,6},{4,7},{9,8},{10,9},{11,1... | collective-permute-start | bytes 13832 | tf_op jit(solution)/shard_map/ppermute | solution.py:26
  199.9 41.5 %collective-permute-start.12 = (f32[1,2,6,96]{3,2,1,0:T(8,128)S(1)}, f32[1,2,6,96]{3,2,1,0:T(8,128)S(1)}, u32[]{:S(2)}, u32[]{:S(2)}) collective-permute-start(f32[1,2,6,96]{3,2,1,0:T(8,128)S(1)} %collective-permute-done.11), channel_id=1, source_target_pairs={{0,1},{1,2},{2,3},{3,0},{4,5},{5,6},{6,7},{7,4},{8,9},{9,10},{10,1... | collective-permute-start | bytes 13832 | tf_op jit(solution)/shard_map/ppermute | solution.py:24
  199.9 41.4 %copy-start.12 = (s32[2,1024,1]{1,0,2:T(2,128)}, s32[2,1024,1]{1,0,2:T(2,128)S(1)}, u32[]{:S(2)}) copy-start(s32[2,1024,1]{1,0,2:T(2,128)S(1)} %iota.19) | copy-start | bytes 24580
  250.6 2.2 copy-start.3
  252.5 2.4 copy-start.8
  255.2 6.7 %collective-permute-start.14 = (f32[1,96,256]{2,0,1:T(1,128)S(1)}, f32[1,96,256]{2,0,1:T(1,128)S(1)}, u32[]{:S(2)}, u32[]{:S(2)}) collective-permute-start(f32[1,96,256]{2,0,1:T(1,128)S(1)} %get-tuple-element.32), channel_id=1, source_target_pairs={{0,4},{4,8},{8,12},{12,16},{16,20},{20,24},{24,28},{1,5},{5,9},{9,... | collective-permute-start | bytes 294920 | tf_op jit(solution)/shard_map/ppermute | solution.py:38
  257.8 4.6 collective-permute-start.15
  259.1 4.9 collective-permute-start.16
  260.4 8.2 %collective-permute-start.17 = (f32[1,2,96,256]{3,0,2,1:T(1,128)S(1)}, f32[1,2,96,256]{3,0,2,1:T(1,128)S(1)}, u32[]{:S(2)}, u32[]{:S(2)}) collective-permute-start(f32[1,2,96,256]{3,0,2,1:T(1,128)S(1)} %get-tuple-element.37), channel_id=1, source_target_pairs={{1,0},{2,1},{3,2},{5,4},{6,5},{7,6},{9,8},{10,9},{11,10},{13,12},{... | collective-permute-start | bytes 589832 | tf_op jit(solution)/shard_map/ppermute | solution.py:41
  262.2 14.4 %copy-start.13 = (s32[2,1024,1]{1,0,2:T(2,128)S(1)}, s32[2,1024,1]{1,0,2:T(2,128)}, u32[]{:S(2)}) copy-start(s32[2,1024,1]{1,0,2:T(2,128)} %copy-done.12) | copy-start | bytes 24580
  262.2 14.4 %copy-start.23 = (s32[2]{0:T(128)S(1)}, s32[2]{0:T(128)}, u32[]{:S(2)}) copy-start(s32[2]{0:T(128)} %constant.96) | copy-start | bytes 28
  262.2 18.1 %copy-start.19 = (pred[2,1024]{1,0:T(4,128)(4,1)S(1)}, pred[2,1024]{1,0:T(4,128)(4,1)}, u32[]{:S(2)}) copy-start(pred[2,1024]{1,0:T(4,128)(4,1)} %and_reduce_fusion) | copy-start | bytes 6148
  272.6 6.3 %collective-permute-start.18 = (f32[1,2,6,96]{3,2,1,0:T(8,128)S(1)}, f32[1,2,6,96]{3,2,1,0:T(8,128)S(1)}, u32[]{:S(2)}, u32[]{:S(2)}) collective-permute-start(f32[1,2,6,96]{3,2,1,0:T(8,128)S(1)} %bitcast.447), channel_id=1, source_target_pairs={{0,1},{1,2},{2,3},{3,0},{4,5},{5,6},{6,7},{7,4},{8,9},{9,10},{10,1... | collective-permute-start | bytes 13832 | tf_op jit(solution)/shard_map/ppermute | solution.py:24
  276.6 44.9 %collective-permute-start.20 = (f32[1,2,6,96]{3,2,1,0:T(8,128)S(1)}, f32[1,2,6,96]{3,2,1,0:T(8,128)S(1)}, u32[]{:S(2)}, u32[]{:S(2)}) collective-permute-start(f32[1,2,6,96]{3,2,1,0:T(8,128)S(1)} %bitcast.448), channel_id=1, source_target_pairs={{1,0},{2,1},{3,2},{0,3},{5,4},{6,5},{7,6},{4,7},{9,8},{10,9},{11,1... | collective-permute-start | bytes 13832 | tf_op jit(solution)/shard_map/ppermute | solution.py:26
  278.9 42.6 %collective-permute-start.19 = (f32[1,2,6,96]{3,2,1,0:T(8,128)S(1)}, f32[1,2,6,96]{3,2,1,0:T(8,128)S(1)}, u32[]{:S(2)}, u32[]{:S(2)}) collective-permute-start(f32[1,2,6,96]{3,2,1,0:T(8,128)S(1)} %collective-permute-done.18), channel_id=1, source_target_pairs={{0,1},{1,2},{2,3},{3,0},{4,5},{5,6},{6,7},{7,4},{8,9},{9,10},{10,1... | collective-permute-start | bytes 13832 | tf_op jit(solution)/shard_map/ppermute | solution.py:24
  334.5 2.2 copy-start.1
  339.1 20.8 %copy-start.25 = (f32[96]{0:T(128)S(1)}, f32[96]{0:T(128)}, u32[]{:S(2)}) copy-start(f32[96]{0:T(128)} %get-tuple-element.12) | copy-start | bytes 1156
  339.1 9.1 %collective-permute-start.21 = (f32[1,96,256]{2,0,1:T(1,128)S(1)}, f32[1,96,256]{2,0,1:T(1,128)S(1)}, u32[]{:S(2)}, u32[]{:S(2)}) collective-permute-start(f32[1,96,256]{2,0,1:T(1,128)S(1)} %get-tuple-element.26), channel_id=1, source_target_pairs={{0,4},{4,8},{8,12},{12,16},{16,20},{20,24},{24,28},{1,5},{5,9},{9,... | collective-permute-start | bytes 294920 | tf_op jit(solution)/shard_map/ppermute | solution.py:38
  341.7 6.9 %collective-permute-start.22 = (f32[1,96,256]{2,0,1:T(1,128)S(1)}, f32[1,96,256]{2,0,1:T(1,128)S(1)}, u32[]{:S(2)}, u32[]{:S(2)}) collective-permute-start(f32[1,96,256]{2,0,1:T(1,128)S(1)} %get-tuple-element.27), channel_id=1, source_target_pairs={{4,0},{8,4},{12,8},{16,12},{20,16},{24,20},{28,24},{5,1},{9,5},{13... | collective-permute-start | bytes 294920 | tf_op jit(solution)/shard_map/ppermute | solution.py:41
  343.0 9.0 %collective-permute-start.23 = (f32[1,2,96,256]{3,0,2,1:T(1,128)S(1)}, f32[1,2,96,256]{3,0,2,1:T(1,128)S(1)}, u32[]{:S(2)}, u32[]{:S(2)}) collective-permute-start(f32[1,2,96,256]{3,0,2,1:T(1,128)S(1)} %get-tuple-element.30), channel_id=1, source_target_pairs={{0,1},{1,2},{2,3},{4,5},{5,6},{6,7},{8,9},{9,10},{10,11},{12,13},{... | collective-permute-start | bytes 589832 | tf_op jit(solution)/shard_map/ppermute | solution.py:38
  346.9 9.5 %collective-permute-start.24 = (f32[1,2,96,256]{3,0,2,1:T(1,128)S(1)}, f32[1,2,96,256]{3,0,2,1:T(1,128)S(1)}, u32[]{:S(2)}, u32[]{:S(2)}) collective-permute-start(f32[1,2,96,256]{3,0,2,1:T(1,128)S(1)} %get-tuple-element.31), channel_id=1, source_target_pairs={{1,0},{2,1},{3,2},{5,4},{6,5},{7,6},{9,8},{10,9},{11,10},{13,12},{... | collective-permute-start | bytes 589832 | tf_op jit(solution)/shard_map/ppermute | solution.py:41
  357.1 48.2 %copy-start.18 = (s32[1,8,2,128]{3,2,1,0:T(2,128)S(1)}, s32[1,8,2,128]{3,2,1,0:T(2,128)}, u32[]{:S(2)}) copy-start(s32[1,8,2,128]{3,2,1,0:T(2,128)} %select_bitcast_fusion.5) | copy-start | bytes 24580
  399.8 5.5 collective-permute-start.25
  401.6 11.8 %collective-permute-start.27 = (f32[1,2,6,96]{3,2,1,0:T(8,128)S(1)}, f32[1,2,6,96]{3,2,1,0:T(8,128)S(1)}, u32[]{:S(2)}, u32[]{:S(2)}) collective-permute-start(f32[1,2,6,96]{3,2,1,0:T(8,128)S(1)} %bitcast.442), channel_id=1, source_target_pairs={{1,0},{2,1},{3,2},{0,3},{5,4},{6,5},{7,6},{4,7},{9,8},{10,9},{11,1... | collective-permute-start | bytes 13832 | tf_op jit(solution)/shard_map/ppermute | solution.py:26
  405.3 8.1 %collective-permute-start.26 = (f32[1,2,6,96]{3,2,1,0:T(8,128)S(1)}, f32[1,2,6,96]{3,2,1,0:T(8,128)S(1)}, u32[]{:S(2)}, u32[]{:S(2)}) collective-permute-start(f32[1,2,6,96]{3,2,1,0:T(8,128)S(1)} %collective-permute-done.25), channel_id=1, source_target_pairs={{0,1},{1,2},{2,3},{3,0},{4,5},{5,6},{6,7},{7,4},{8,9},{9,10},{10,1... | collective-permute-start | bytes 13832 | tf_op jit(solution)/shard_map/ppermute | solution.py:24
  424.8 2.8 copy-start.4
  429.3 17.1 %copy-start.6 = (f32[2,96,1024]{2,1,0:T(8,128)}, f32[2,96,1024]{2,1,0:T(8,128)S(1)}, u32[]{:S(2)}) copy-start(f32[2,96,1024]{2,1,0:T(8,128)S(1)} %fusion) | copy-start | bytes 2359300
  430.0 7.7 %collective-permute-start.28 = (f32[1,96,256]{2,0,1:T(1,128)S(1)}, f32[1,96,256]{2,0,1:T(1,128)S(1)}, u32[]{:S(2)}, u32[]{:S(2)}) collective-permute-start(f32[1,96,256]{2,0,1:T(1,128)S(1)} %get-tuple-element.20), channel_id=1, source_target_pairs={{0,4},{4,8},{8,12},{12,16},{16,20},{20,24},{24,28},{1,5},{5,9},{9,... | collective-permute-start | bytes 294920 | tf_op jit(solution)/shard_map/ppermute | solution.py:38
  432.6 5.5 collective-permute-start.29
  433.9 7.0 %collective-permute-start.30 = (f32[1,2,96,256]{3,0,2,1:T(1,128)S(1)}, f32[1,2,96,256]{3,0,2,1:T(1,128)S(1)}, u32[]{:S(2)}, u32[]{:S(2)}) collective-permute-start(f32[1,2,96,256]{3,0,2,1:T(1,128)S(1)} %get-tuple-element.24), channel_id=1, source_target_pairs={{0,1},{1,2},{2,3},{4,5},{5,6},{6,7},{8,9},{9,10},{10,11},{12,13},{... | collective-permute-start | bytes 589832 | tf_op jit(solution)/shard_map/ppermute | solution.py:38
  436.4 9.3 %collective-permute-start.31 = (f32[1,2,96,256]{3,0,2,1:T(1,128)S(1)}, f32[1,2,96,256]{3,0,2,1:T(1,128)S(1)}, u32[]{:S(2)}, u32[]{:S(2)}) collective-permute-start(f32[1,2,96,256]{3,0,2,1:T(1,128)S(1)} %get-tuple-element.25), channel_id=1, source_target_pairs={{1,0},{2,1},{3,2},{5,4},{6,5},{7,6},{9,8},{10,9},{11,10},{13,12},{... | collective-permute-start | bytes 589832 | tf_op jit(solution)/shard_map/ppermute | solution.py:41
  437.9 58.8 %copy-start.27 = (f32[96]{0:T(128)S(1)}, f32[96]{0:T(128)}, u32[]{:S(2)}) copy-start(f32[96]{0:T(128)} %copy-done.26) | copy-start | bytes 1156
  450.4 5.5 collective-permute-start.32
  452.5 44.2 %collective-permute-start.34 = (f32[1,2,6,96]{3,2,1,0:T(8,128)S(1)}, f32[1,2,6,96]{3,2,1,0:T(8,128)S(1)}, u32[]{:S(2)}, u32[]{:S(2)}) collective-permute-start(f32[1,2,6,96]{3,2,1,0:T(8,128)S(1)} %bitcast.451), channel_id=1, source_target_pairs={{1,0},{2,1},{3,2},{0,3},{5,4},{6,5},{7,6},{4,7},{9,8},{10,9},{11,1... | collective-permute-start | bytes 13832 | tf_op jit(solution)/shard_map/ppermute | solution.py:26
  455.9 40.9 %collective-permute-start.33 = (f32[1,2,6,96]{3,2,1,0:T(8,128)S(1)}, f32[1,2,6,96]{3,2,1,0:T(8,128)S(1)}, u32[]{:S(2)}, u32[]{:S(2)}) collective-permute-start(f32[1,2,6,96]{3,2,1,0:T(8,128)S(1)} %collective-permute-done.32), channel_id=1, source_target_pairs={{0,1},{1,2},{2,3},{3,0},{4,5},{5,6},{6,7},{7,4},{8,9},{9,10},{10,1... | collective-permute-start | bytes 13832 | tf_op jit(solution)/shard_map/ppermute | solution.py:24
  515.3 61.0 %copy-start.29 = (f32[96]{0:T(128)S(1)}, f32[96]{0:T(128)}, u32[]{:S(2)}) copy-start(f32[96]{0:T(128)} %copy-done.28) | copy-start | bytes 1156
  515.3 61.0 %copy-start.22 = (f32[96]{0:T(128)S(1)}, f32[96]{0:T(128)}, u32[]{:S(2)}) copy-start(f32[96]{0:T(128)} %copy-done.21) | copy-start | bytes 1156
  515.3 8.2 %collective-permute-start.35 = (f32[1,96,256]{2,0,1:T(1,128)S(1)}, f32[1,96,256]{2,0,1:T(1,128)S(1)}, u32[]{:S(2)}, u32[]{:S(2)}) collective-permute-start(f32[1,96,256]{2,0,1:T(1,128)S(1)} %get-tuple-element.14), channel_id=1, source_target_pairs={{0,4},{4,8},{8,12},{12,16},{16,20},{20,24},{24,28},{1,5},{5,9},{9,... | collective-permute-start | bytes 294920 | tf_op jit(solution)/shard_map/ppermute | solution.py:38
  517.9 6.0 collective-permute-start.36
  519.2 6.8 %collective-permute-start.37 = (f32[1,2,96,256]{3,0,2,1:T(1,128)S(1)}, f32[1,2,96,256]{3,0,2,1:T(1,128)S(1)}, u32[]{:S(2)}, u32[]{:S(2)}) collective-permute-start(f32[1,2,96,256]{3,0,2,1:T(1,128)S(1)} %get-tuple-element.18), channel_id=1, source_target_pairs={{0,1},{1,2},{2,3},{4,5},{5,6},{6,7},{8,9},{9,10},{10,11},{12,13},{... | collective-permute-start | bytes 589832 | tf_op jit(solution)/shard_map/ppermute | solution.py:38
  522.1 8.6 %collective-permute-start.38 = (f32[1,2,96,256]{3,0,2,1:T(1,128)S(1)}, f32[1,2,96,256]{3,0,2,1:T(1,128)S(1)}, u32[]{:S(2)}, u32[]{:S(2)}) collective-permute-start(f32[1,2,96,256]{3,0,2,1:T(1,128)S(1)} %get-tuple-element.19), channel_id=1, source_target_pairs={{1,0},{2,1},{3,2},{5,4},{6,5},{7,6},{9,8},{10,9},{11,10},{13,12},{... | collective-permute-start | bytes 589832 | tf_op jit(solution)/shard_map/ppermute | solution.py:41
  594.6 13.4 %copy-start.5 = (f32[2,1024,96]{1,2,0:T(8,128)S(1)}, f32[2,1024,96]{1,2,0:T(8,128)}, u32[]{:S(2)}) copy-start(f32[2,1024,96]{1,2,0:T(8,128)} %copy.108) | copy-start | bytes 2359300
  (5 other events, 4.7 us)
